TPU v7x, 128 devices: a whole 4x4x4 slice. The times are simulated.
128 devices in a mesh: gx: 8 (over y_hi, z), gy: 16 (over x, y_lo, core).
Axes of the slice: x: 4, y: 4 (y_hi: 2, y_lo: 2; y = y_hi * 2 + y_lo), z: 4, core: 2. Of those that a mesh axis runs over, the one named last changes fastest.
Arguments:
- observed: float32 [2, 8192, 8192], P(None, 'gx', 'gy'), may hold values from -6 to 6
- noise_var: float32 [8192, 8192], P('gx', 'gy'), may hold values from 0.05 to 0.5
- row_kernel: float32 [4096, 4096], P('gx'), may hold values from -1 to 1.2, as said below
- col_kernel: float32 [4096, 4096], P('gy'), may hold values from -1 to 1.2, as said below
Outputs:
- gram_times: float32 [2, 8192, 8192], P(None, 'gx', 'gy')
Inputs may be any that keep to these rules, and one draw needn't show every extreme that they name: row_kernel is symmetric. col_kernel is symmetric.
All inputs are finite; a program needn't handle non-finite values.
Results may differ from a plain program's by a relative error of at most 0.000065.
Values sent between devices are 32-bit elements; how exact they have to be, the bound alone decides.
No kernel may reach another device: no remote copies, remote signals or barrier semaphores. Data moves between devices by JAX's collectives and lax.ppermute only.
A program may use at most 128 MiB of HBM per device.

v0:
```python
import jax
import jax.numpy as jnp
from jax import lax
from jax.sharding import PartitionSpec as P

even_taps = (-0.0703125, 0.8671875, 0.2265625, -0.0234375)
odd_taps = (-0.0234375, 0.2265625, 0.8671875, -0.0703125)


def with_halo(cells, sides, width):
    for axis, dim in sides:
        count = lax.axis_size(axis)
        ends = count - 1
        head = lax.slice_in_dim(cells, 0, width, axis=dim)
        tail = lax.slice_in_dim(cells, cells.shape[dim] - width, cells.shape[dim], axis=dim)
        cells = jnp.concatenate(
            [
                lax.ppermute(tail, axis, [(i, (i + 1) % count) for i in range(ends)]),
                cells,
                lax.ppermute(head, axis, [((i + 1) % count, i) for i in range(ends)]),
            ],
            axis=dim,
        )
    return cells


def keys_weight(dist):
    span = jnp.abs(dist)
    inner = (1.5 * span - 2.5) * span * span + 1.0
    outer = ((-0.5 * span + 2.5) * span - 4.0) * span + 2.0
    return jnp.where(span < 1.0, inner, jnp.where(span < 2.0, outer, 0.0))


def adjoint_rows(extended, count):
    evens = extended[:, 0::2]
    odds = extended[:, 1::2]
    total = jnp.zeros((extended.shape[0], count, extended.shape[2]), jnp.float32)
    for index in range(4):
        start = 3 - index
        total = (
            total
            + even_taps[index] * evens[:, start : start + count]
            + odd_taps[index] * odds[:, start : start + count]
        )
    return total


def forward_rows(extended, count):
    first = jnp.zeros((extended.shape[0], count, extended.shape[2]), jnp.float32)
    second = jnp.zeros((extended.shape[0], count, extended.shape[2]), jnp.float32)
    for index in range(4):
        start = index + 1
        first = first + even_taps[index] * extended[:, start : start + count]
        second = second + odd_taps[index] * extended[:, start : start + count]
    stacked = jnp.stack([first, second], axis=2)
    return stacked.reshape(extended.shape[0], 2 * count, extended.shape[2])


def body(observed, noise_var, row_kernel, col_kernel):
    highest = lax.Precision.HIGHEST
    tile_rows = row_kernel.shape[0]
    tile_cols = col_kernel.shape[0]
    extended = with_halo(observed, (("gx", 1), ("gy", 2)), 4)
    rowsum = adjoint_rows(extended, tile_rows)
    fine_index = lax.broadcasted_iota(jnp.float32, (2 * tile_cols + 8, tile_cols), 0)
    coarse_index = lax.broadcasted_iota(jnp.float32, (2 * tile_cols + 8, tile_cols), 1)
    adjoint_table = keys_weight(coarse_index - ((fine_index - 4.0) * 0.5 + 0.25))
    inducing = jnp.einsum("riq,qj->rij", rowsum, adjoint_table, precision=highest)
    block = col_kernel
    mixed = jnp.einsum(
        "rik,jk->rij", lax.all_gather(inducing, "gy", axis=2, tiled=True), block, precision=highest
    )
    block = row_kernel
    product = jnp.einsum(
        "ik,rkj->rij", block, lax.all_gather(mixed, "gx", axis=1, tiled=True), precision=highest
    )
    coarse_ext = with_halo(product, (("gx", 1), ("gy", 2)), 2)
    coarse_pos = lax.broadcasted_iota(jnp.float32, (tile_cols + 4, 2 * tile_cols), 0)
    fine_pos = lax.broadcasted_iota(jnp.float32, (tile_cols + 4, 2 * tile_cols), 1)
    forward_table = keys_weight(coarse_pos - 2.0 - (fine_pos * 0.5 + 0.25))
    colpass = jnp.einsum("riq,qp->rip", coarse_ext, forward_table, precision=highest)
    result = forward_rows(colpass, tile_rows)
    return result + noise_var[None] * observed


def solution(mesh):
    return jax.shard_map(
        body,
        mesh=mesh,
        in_specs=(P(None, "gx", "gy"), P("gx", "gy"), P("gx", None), P("gy", None)),
        out_specs=P(None, "gx", "gy"),
        check_vma=False,
    )
```

profile of v0, /device:TPU:1, one launch (start us, length us, event | category | flops | bytes accessed | tf_op | source)
XLA Modules:
  0.0 501.1 jit_solution(13943652299818012034)
XLA Ops:
  6.5 0.0 all-gather.3.cloned.1.call-start
  6.5 0.8 fusion.111
  7.3 0.2 copy.15
  7.5 4.4 collective-permute-start
  12.0 0.2 copy.16
  12.2 1.3 collective-permute-start.1
  13.5 5.4 %copy.17 = f32[2,1024,512]{1,2,0:T(8,128)} copy(f32[2,1024,512]{2,1,0:T(8,128)} %param.4) | data formatting | bytes 8388608 | tf_op args[0]
  18.8 3.7 collective-permute-done
  22.5 4.4 collective-permute-done.1
  26.9 6.4 %concatenate.12 = f32[2,1032,512]{1,2,0:T(8,128)} concatenate(f32[2,4,512]{1,2,0:T(8,128)S(1)} %collective-permute-done, f32[2,1024,512]{1,2,0:T(8,128)} %copy.17, f32[2,4,512]{1,2,0:T(8,128)S(1)} %collective-permute-done.1), dimensions={1} | concatenate | bytes 8454144 | tf_op jit(solution)/shard_map/concatenate | solution.py:16
  33.3 0.9 fusion.110
  34.3 4.8 collective-permute-start.2
  39.1 1.9 collective-permute-start.3
  41.0 0.0 collective-permute-done.2
  41.0 3.3 collective-permute-done.3
  44.3 4.8 pad_maximum_fusion
  49.2 74.3 %slice.74 = f32[2,516,520]{1,2,0:T(8,128)S(1)} slice(f32[2,1032,520]{1,2,0:T(8,128)} %pad_maximum_fusion), slice={[0:2:1], [0:1032:2], [0:520:1]} | slice | bytes 4293120 | tf_op jit(solution)/shard_map/slice | solution.py:35
  123.4 74.5 %slice.76 = f32[2,516,520]{1,2,0:T(8,128)} slice(f32[2,1032,520]{1,2,0:T(8,128)} %pad_maximum_fusion), slice={[0:2:1], [1:1032:2], [0:520:1]} | slice | bytes 4293120 | tf_op jit(solution)/shard_map/slice | solution.py:36
  198.0 13.2 %fusion.5 = f32[2,512,256]{2,1,0:T(8,128)} fusion(f32[2,516,520]{1,2,0:T(8,128)} %slice.76, f32[2,516,520]{1,2,0:T(8,128)S(1)} %slice.74, f32[520]{0:T(1024)S(1)} %multiply_add_fusion), kind=kOutput, calls=%fused_computation.9 | convolution fusion | flops 1646028800 | bytes 18092032 | tf_op jit(solution)/shard_map/riq,qj->rij/dot_general | solution.py:68
  211.2 0.0 all-gather.3.cloned.1.call-update
  211.2 0.2 all-gather.5.cloned.1.call-start
  211.4 95.9 %all-gather.3.cloned.1.call-done = f32[2,512,4096]{2,1,0:T(8,128)} async-done(((f32[2,512,256]{2,1,0:T(8,128)}), f32[2,512,4096]{2,1,0:T(8,128)}) %all-gather.3.cloned.1.call-update) | async-done | bytes 16777232 | tf_op jit(solution)/shard_map/all_gather | solution.py:71
  307.3 17.3 %fusion.2 = f32[2,512,256]{2,1,0:T(8,128)} fusion(f32[2,512,4096]{2,1,0:T(8,128)} %all-gather.3.cloned.1.call-done, f32[256,4096]{1,0:T(8,128)} %param.7), kind=kOutput, calls=%fused_computation.4 | convolution fusion | flops 12884901888 | bytes 22020096 | tf_op jit(solution)/shard_map/rik,jk->rij/dot_general | solution.py:70
  324.6 0.0 all-gather.5.cloned.1.call-update
  324.6 107.4 %all-gather.5.cloned.1.call-done = f32[2,4096,256]{2,1,0:T(8,128)} async-done(((f32[2,512,256]{2,1,0:T(8,128)}), f32[2,4096,256]{2,1,0:T(8,128)}) %all-gather.5.cloned.1.call-update) | async-done | bytes 8388624 | tf_op jit(solution)/shard_map/all_gather | solution.py:75
  432.1 29.2 %fusion.19 = f32[2,512,256]{1,2,0:T(8,128)S(1)} fusion(f32[2,4096,256]{2,1,0:T(8,128)} %all-gather.5.cloned.1.call-done, f32[512,4096]{1,0:T(8,128)} %param.6), kind=kOutput, calls=%fused_computation.25 | convolution fusion | flops 12884901888 | bytes 17825792 | tf_op jit(solution)/shard_map/ik,rkj->rij/dot_general | solution.py:74
  461.3 0.1 fusion.112
  461.4 1.8 collective-permute-start.4
  463.2 1.3 collective-permute-start.5
  464.6 3.2 collective-permute-done.4
  467.7 3.8 collective-permute-done.5
  471.6 0.1 pad_maximum_fusion.4
  471.7 4.4 collective-permute-start.6
  476.1 2.1 collective-permute-start.7
  478.2 0.0 collective-permute-done.6
  478.2 2.8 collective-permute-done.7
  481.1 4.6 fusion.22
  485.7 1.5 add_bitcast_fusion.1
  487.2 0.4 pad_maximum_fusion.1
  487.6 0.0 copy-start
  487.6 0.0 copy-start.1
  487.6 3.2 copy.19
  490.9 0.0 copy-done
  490.9 0.0 copy-done.1
  490.9 3.3 copy_add_fusion
  (3 shorter events, 0.0 us)
Async XLA Ops:
  6.5 300.8 %all-gather.3.cloned.1.call-start = ((), (), s32[]{:S(2)}) async-start(), calls=%async_computation | async-start | bytes 17825792 | tf_op jit(solution)/shard_map/all_gather | solution.py:71
  7.5 15.0 %collective-permute-start = (f32[2,4,512]{1,2,0:T(8,128)S(1)}, f32[2,4,512]{1,2,0:T(8,128)S(1)}, u32[]{:S(2)}, u32[]{:S(2)}) collective-permute-start(f32[2,4,512]{1,2,0:T(8,128)S(1)} %copy.15), channel_id=1, source_target_pairs={{0,16},{16,32},{32,48},{48,64},{64,80},{80,96},{96,112},{1,17},{17... | collective-permute-start | bytes 49160 | tf_op jit(solution)/shard_map/ppermute | solution.py:18
  12.2 14.7 %collective-permute-start.1 = (f32[2,4,512]{1,2,0:T(8,128)S(1)}, f32[2,4,512]{1,2,0:T(8,128)S(1)}, u32[]{:S(2)}, u32[]{:S(2)}) collective-permute-start(f32[2,4,512]{1,2,0:T(8,128)S(1)} %copy.16), channel_id=1, source_target_pairs={{16,0},{32,16},{48,32},{64,48},{80,64},{96,80},{112,96},{17,1},{33... | collective-permute-start | bytes 49160 | tf_op jit(solution)/shard_map/ppermute | solution.py:20
  34.3 6.7 %collective-permute-start.2 = (f32[2,1032,4]{1,2,0:T(4,128)S(1)}, f32[2,1032,4]{1,2,0:T(4,128)S(1)}, u32[]{:S(2)}, u32[]{:S(2)}) collective-permute-start(f32[2,1032,4]{1,2,0:T(4,128)S(1)} %get-tuple-element.5), channel_id=1, source_target_pairs={{0,1},{1,2},{2,3},{3,4},{4,5},{5,6},{6,7},{7,8},{8,9},{9,10},{10,1... | collective-permute-start | bytes 99080 | tf_op jit(solution)/shard_map/ppermute | solution.py:18
  39.1 5.3 %collective-permute-start.3 = (f32[2,1032,4]{1,2,0:T(4,128)S(1)}, f32[2,1032,4]{1,2,0:T(4,128)S(1)}, u32[]{:S(2)}, u32[]{:S(2)}) collective-permute-start(f32[2,1032,4]{1,2,0:T(4,128)S(1)} %get-tuple-element.6), channel_id=1, source_target_pairs={{1,0},{2,1},{3,2},{4,3},{5,4},{6,5},{7,6},{8,7},{9,8},{10,9},{11,1... | collective-permute-start | bytes 99080 | tf_op jit(solution)/shard_map/ppermute | solution.py:20
  211.2 220.9 %all-gather.5.cloned.1.call-start = ((), (), s32[]{:S(2)}) async-start(), calls=%async_computation.1 | async-start | bytes 9437184 | tf_op jit(solution)/shard_map/all_gather | solution.py:75
  461.4 6.3 %collective-permute-start.4 = (f32[2,2,256]{1,2,0:T(8,128)S(1)}, f32[2,2,256]{1,2,0:T(8,128)S(1)}, u32[]{:S(2)}, u32[]{:S(2)}) collective-permute-start(f32[2,2,256]{1,2,0:T(8,128)S(1)} %get-tuple-element.13), channel_id=1, source_target_pairs={{0,16},{16,32},{32,48},{48,64},{64,80},{80,96},{96,112},{1,17},{17... | collective-permute-start | bytes 12296 | tf_op jit(solution)/shard_map/ppermute | solution.py:18
  463.2 8.3 %collective-permute-start.5 = (f32[2,2,256]{1,2,0:T(8,128)S(1)}, f32[2,2,256]{1,2,0:T(8,128)S(1)}, u32[]{:S(2)}, u32[]{:S(2)}) collective-permute-start(f32[2,2,256]{1,2,0:T(8,128)S(1)} %get-tuple-element.14), channel_id=1, source_target_pairs={{16,0},{32,16},{48,32},{64,48},{80,64},{96,80},{112,96},{17,1},{33... | collective-permute-start | bytes 12296 | tf_op jit(solution)/shard_map/ppermute | solution.py:20
  471.7 6.6 %collective-permute-start.6 = (f32[2,516,2]{1,2,0:T(2,128)S(1)}, f32[2,516,2]{1,2,0:T(2,128)S(1)}, u32[]{:S(2)}, u32[]{:S(2)}) collective-permute-start(f32[2,516,2]{1,2,0:T(2,128)S(1)} %get-tuple-element.11), channel_id=1, source_target_pairs={{0,1},{1,2},{2,3},{3,4},{4,5},{5,6},{6,7},{7,8},{8,9},{9,10},{10,1... | collective-permute-start | bytes 24776 | tf_op jit(solution)/shard_map/ppermute | solution.py:18
  476.1 5.0 collective-permute-start.7
  487.6 3.3 copy-start
  487.6 3.3 copy-start.1
Sparse Core Ops, SparseCore 0:
  211.3 95.9 all-gather.2
  324.8 107.2 all-gather.4
where the time goes:
time: 505 us; the launch traced here: 501 us
  waiting for transfers between devices  225 us (45%)
  local copies, waits for them, and re-layouts  166 us (33%)
  matrix products  64.3 us (13%)
  starting transfers between devices  22.2 us (4%)
  between operations  13.6 us (3%)
  other arithmetic  10.2 us (2%)
    all_gather x1, waiting for transfers between devices, body(): lax.all_gather(mixed, 'gx', axis=1, tiled=True)  107 us
    all_gather x1, waiting for transfers between devices, body(): lax.all_gather(inducing, 'gy', axis=2, tiled=True)  95.9 us
    slice x1, local copies, waits for them, and re-layouts, adjoint_rows(): odds = extended[:, 1::2]  74.5 us
    slice x1, local copies, waits for them, and re-layouts, adjoint_rows(): evens = extended[:, 0::2]  74.3 us
    dot_general x1, matrix products, body(): jnp.einsum('ik,rkj->rij', block, lax.all_gather(mixed, 'gx', axis=1, tile...  29.2 us
    dot_general x1, matrix products, body(): jnp.einsum('rik,jk->rij', lax.all_gather(inducing, 'gy', axis=2, tiled=Tr...  17.3 us
    ppermute x4, starting transfers between devices, with_halo(): lax.ppermute(tail, axis, [(i, (i + 1) % count) for i in range(ends)])  15.4 us
    ppermute x4, waiting for transfers between devices, with_halo(): lax.ppermute(head, axis, [((i + 1) % count, i) for i in range(ends)])  14.4 us
  transfers between devices with their start and end apart: 10, of which 8 were waited for; matrix products, arithmetic and copies ran while one was open for 1% of the time, Pallas kernels for 0%

commit v1 on v0

v1 whole, which is shorter than its diff:
```python
import jax
import jax.numpy as jnp
from jax import lax
from jax.sharding import PartitionSpec as P


def with_halo(cells, sides, width):
    for axis, dim in sides:
        count = lax.axis_size(axis)
        ends = count - 1
        head = lax.slice_in_dim(cells, 0, width, axis=dim)
        tail = lax.slice_in_dim(cells, cells.shape[dim] - width, cells.shape[dim], axis=dim)
        cells = jnp.concatenate(
            [
                lax.ppermute(tail, axis, [(i, (i + 1) % count) for i in range(ends)]),
                cells,
                lax.ppermute(head, axis, [((i + 1) % count, i) for i in range(ends)]),
            ],
            axis=dim,
        )
    return cells


def keys_weight(dist):
    span = jnp.abs(dist)
    inner = (1.5 * span - 2.5) * span * span + 1.0
    outer = ((-0.5 * span + 2.5) * span - 4.0) * span + 2.0
    return jnp.where(span < 1.0, inner, jnp.where(span < 2.0, outer, 0.0))


def tap_table(rows, cols, coarse_on_rows, pad):
    r = lax.broadcasted_iota(jnp.float32, (rows, cols), 0)
    c = lax.broadcasted_iota(jnp.float32, (rows, cols), 1)
    if coarse_on_rows:
        coarse, fine = r, c
    else:
        coarse, fine = c, r
    if pad == 4:
        dist = coarse - ((fine - 4.0) * 0.5 + 0.25)
    else:
        dist = coarse - 2.0 - (fine * 0.5 + 0.25)
    return keys_weight(dist).astype(jnp.bfloat16)


def split3(x):
    hi = lax.reduce_precision(x, exponent_bits=8, mantissa_bits=7)
    rest = x - hi
    mid = lax.reduce_precision(rest, exponent_bits=8, mantissa_bits=7)
    lo = rest - mid
    return hi.astype(jnp.bfloat16), mid.astype(jnp.bfloat16), lo.astype(jnp.bfloat16)


def exact_dot(eq, x, table, data_first):
    total = None
    for part in split3(x):
        if data_first:
            term = jnp.einsum(eq, part, table, preferred_element_type=jnp.float32)
        else:
            term = jnp.einsum(eq, table, part, preferred_element_type=jnp.float32)
        total = term if total is None else total + term
    return total


def body(observed, noise_var, row_kernel, col_kernel):
    highest = lax.Precision.HIGHEST
    tile_rows = row_kernel.shape[0]
    tile_cols = col_kernel.shape[0]
    extended = with_halo(observed, (("gx", 1), ("gy", 2)), 4)
    col_adj = tap_table(2 * tile_cols + 8, tile_cols, False, 4)
    row_adj = tap_table(tile_rows, 2 * tile_rows + 8, True, 4)
    colsum = exact_dot("rpq,qj->rpj", extended, col_adj, True)
    inducing = exact_dot("ip,rpj->rij", colsum, row_adj, False)
    mixed = jnp.einsum(
        "rik,jk->rij", lax.all_gather(inducing, "gy", axis=2, tiled=True), col_kernel, precision=highest
    )
    product = jnp.einsum(
        "ik,rkj->rij", row_kernel, lax.all_gather(mixed, "gx", axis=1, tiled=True), precision=highest
    )
    coarse_ext = with_halo(product, (("gx", 1), ("gy", 2)), 2)
    row_fwd = tap_table(2 * tile_rows, tile_rows + 4, False, 2)
    col_fwd = tap_table(tile_cols + 4, 2 * tile_cols, True, 2)
    rowpass = exact_dot("pi,rij->rpj", coarse_ext, row_fwd, False)
    result = exact_dot("rpj,jq->rpq", rowpass, col_fwd, True)
    return result + noise_var[None] * observed


def solution(mesh):
    return jax.shard_map(
        body,
        mesh=mesh,
        in_specs=(P(None, "gx", "gy"), P("gx", "gy"), P("gx", None), P("gy", None)),
        out_specs=P(None, "gx", "gy"),
        check_vma=False,
    )
```

time: 505 us -> 344 us (0.68)
  local copies, waits for them, and re-layouts: 166 us -> 15.2 us
  other arithmetic: 10.2 us -> 0.15 us
    slice x2 -> x0, local copies, waits for them, and re-layouts: 149 us -> none  [the longest x1 74.5 us: adjoint_rows(): odds = extended[:, 1::2]]
    dot_general x3 -> x13, matrix products: 47 us -> 45.9 us  [the longest x1 16.5 us: body(): jnp.einsum('ik,rkj->rij', row_kernel, lax.all_gather(mixed, 'gx', axis=1,...]
  transfers between devices with their start and end apart: 10 -> 10, of which waited for: 8 -> 8; matrix products, arithmetic and copies ran while one was open for 1% -> 2% of each run, Pallas kernels for 0% -> 0%
where the time goes in v1:
time: 344 us; the launch traced here: 340 us
  waiting for transfers between devices  224 us (65%)
  matrix products  64.6 us (19%)
  starting transfers between devices  22.2 us (6%)
  local copies, waits for them, and re-layouts  15.2 us (4%)
  between operations  13.7 us (4%)
    all_gather x1, waiting for transfers between devices, body(): lax.all_gather(mixed, 'gx', axis=1, tiled=True)  107 us
    all_gather x1, waiting for transfers between devices, body(): lax.all_gather(inducing, 'gy', axis=2, tiled=True)  95.9 us
    dot_general x1, matrix products, body(): jnp.einsum('rik,jk->rij', lax.all_gather(inducing, 'gy', axis=2, tiled=Tr...  18.7 us
    dot_general x1, matrix products, body(): jnp.einsum('ik,rkj->rij', row_kernel, lax.all_gather(mixed, 'gx', axis=1,...  16.5 us
    ppermute x4, starting transfers between devices, with_halo(): lax.ppermute(tail, axis, [(i, (i + 1) % count) for i in range(ends)])  15.4 us
    dot_general x6, matrix products, exact_dot(): term = jnp.einsum(eq, part, table, preferred_element_type=jnp.float32)  15.4 us
    ppermute x4, waiting for transfers between devices, with_halo(): lax.ppermute(head, axis, [((i + 1) % count, i) for i in range(ends)])  14.4 us
    dot_general x6, matrix products, exact_dot(): term = jnp.einsum(eq, table, part, preferred_element_type=jnp.float32)  14 us
  transfers between devices with their start and end apart: 10, of which 8 were waited for; matrix products, arithmetic and copies ran while one was open for 2% of the time, Pallas kernels for 0%

profile of v1, /device:TPU:1, one launch (start us, length us, event | category | flops | bytes accessed | tf_op | source)
XLA Modules:
  0.0 340.3 jit_solution(4553830211011986226)
XLA Ops:
  6.5 0.0 all-gather.3.cloned.1.call-start
  6.5 0.8 fusion.196
  7.3 0.2 copy.5
  7.5 4.4 %collective-permute-start = (f32[2,4,512]{1,2,0:T(8,128)S(1)}, f32[2,4,512]{1,2,0:T(8,128)S(1)}, u32[]{:S(2)}, u32[]{:S(2)}) collective-permute-start(f32[2,4,512]{1,2,0:T(8,128)S(1)} %copy.5), channel_id=1, source_target_pairs={{0,16},{16,32},{32,48},{48,64},{64,80},{80,96},{96,112},{1,17},{17... | collective-permute-start | bytes 49160 | tf_op jit(solution)/shard_map/ppermute | solution.py:15
  12.0 0.2 copy.6
  12.2 1.3 collective-permute-start.1
  13.5 5.4 %copy.7 = f32[2,1024,512]{1,2,0:T(8,128)} copy(f32[2,1024,512]{2,1,0:T(8,128)} %param.4) | data formatting | bytes 8388608 | tf_op args[0]
  18.9 3.6 %collective-permute-done = f32[2,4,512]{1,2,0:T(8,128)S(1)} collective-permute-done((f32[2,4,512]{1,2,0:T(8,128)S(1)}, f32[2,4,512]{1,2,0:T(8,128)S(1)}, u32[]{:S(2)}, u32[]{:S(2)}) %collective-permute-start) | collective-permute-done | bytes 16416 | tf_op jit(solution)/shard_map/ppermute | solution.py:15
  22.5 4.4 %collective-permute-done.1 = f32[2,4,512]{1,2,0:T(8,128)S(1)} collective-permute-done((f32[2,4,512]{1,2,0:T(8,128)S(1)}, f32[2,4,512]{1,2,0:T(8,128)S(1)}, u32[]{:S(2)}, u32[]{:S(2)}) %collective-permute-start.1) | collective-permute-done | bytes 16416 | tf_op jit(solution)/shard_map/ppermute | solution.py:17
  26.9 6.4 %concatenate.12 = f32[2,1032,512]{1,2,0:T(8,128)} concatenate(f32[2,4,512]{1,2,0:T(8,128)S(1)} %collective-permute-done, f32[2,1024,512]{1,2,0:T(8,128)} %copy.7, f32[2,4,512]{1,2,0:T(8,128)S(1)} %collective-permute-done.1), dimensions={1} | concatenate | bytes 8454144 | tf_op jit(solution)/shard_map/concatenate | solution.py:13
  33.3 0.9 fusion.195
  34.2 4.8 %collective-permute-start.2 = (f32[2,1032,4]{1,2,0:T(4,128)S(1)}, f32[2,1032,4]{1,2,0:T(4,128)S(1)}, u32[]{:S(2)}, u32[]{:S(2)}) collective-permute-start(f32[2,1032,4]{1,2,0:T(4,128)S(1)} %get-tuple-element.5), channel_id=1, source_target_pairs={{0,1},{1,2},{2,3},{3,4},{4,5},{5,6},{6,7},{7,8},{8,9},{9,10},{10,1... | collective-permute-start | bytes 99080 | tf_op jit(solution)/shard_map/ppermute | solution.py:15
  39.0 1.9 collective-permute-start.3
  40.9 0.0 slice-start
  40.9 0.0 slice-start.1
  41.0 0.0 collective-permute-done.2
  41.0 3.3 collective-permute-done.3
  44.3 4.0 %fusion.8 = f32[2,1032,256]{2,1,0:T(8,128)S(1)} fusion(f32[2,1032,4]{1,2,0:T(4,128)S(1)} %collective-permute-done.3, f32[2,1032,512]{1,2,0:T(8,128)} %concatenate.12, f32[2,1032,4]{1,2,0:T(4,128)S(1)} %collective-permute-done.2, f32[520]{0:T(1024)S(1)} %multiply_add_fusion.3), kind=kOutput, calls=%fused_computation.24 | convolution fusion | flops 558355200 | bytes 6408736 | tf_op jit(solution)/shard_map/rpq,qj->rpj/dot_general | solution.py:57
  48.2 0.0 slice-done
  48.2 0.0 slice-done.1
  48.3 1.9 fusion.6
  50.2 1.6 fusion.5
  51.8 2.0 fusion.29
  53.8 2.2 convolution_add_fusion.2
  55.9 3.3 fusion.24
  59.2 0.0 all-gather.3.cloned.1.call-update
  59.2 0.2 all-gather.5.cloned.1.call-start
  59.4 95.9 %all-gather.3.cloned.1.call-done = f32[2,512,4096]{1,2,0:T(8,128)} async-done(((f32[2,512,256]{1,2,0:T(8,128)}), f32[2,512,4096]{1,2,0:T(8,128)}) %all-gather.3.cloned.1.call-update) | async-done | bytes 16777232 | tf_op jit(solution)/shard_map/all_gather | solution.py:74
  155.4 18.7 %fusion.3 = f32[2,512,256]{1,2,0:T(8,128)} fusion(f32[2,512,4096]{1,2,0:T(8,128)} %all-gather.3.cloned.1.call-done, f32[256,4096]{1,0:T(8,128)} %param.7), kind=kOutput, calls=%fused_computation.8 | convolution fusion | flops 12884901888 | bytes 22020096 | tf_op jit(solution)/shard_map/rik,jk->rij/dot_general | solution.py:73
  174.0 0.0 all-gather.5.cloned.1.call-update
  174.1 107.4 %all-gather.5.cloned.1.call-done = f32[2,4096,256]{1,2,0:T(8,128)} async-done(((f32[2,512,256]{1,2,0:T(8,128)}), f32[2,4096,256]{1,2,0:T(8,128)}) %all-gather.5.cloned.1.call-update) | async-done | bytes 8388624 | tf_op jit(solution)/shard_map/all_gather | solution.py:77
  281.5 16.5 %fusion.21 = f32[2,512,256]{1,2,0:T(8,128)S(1)} fusion(f32[2,4096,256]{1,2,0:T(8,128)} %all-gather.5.cloned.1.call-done, f32[512,4096]{1,0:T(8,128)} %param.6), kind=kOutput, calls=%fused_computation.44 | convolution fusion | flops 12884901888 | bytes 17825792 | tf_op jit(solution)/shard_map/ik,rkj->rij/dot_general | solution.py:76
  297.9 0.1 fusion.197
  298.1 1.8 collective-permute-start.4
  299.9 1.3 collective-permute-start.5
  301.2 3.2 collective-permute-done.4
  304.4 3.8 %collective-permute-done.5 = f32[2,2,256]{1,2,0:T(8,128)S(1)} collective-permute-done((f32[2,2,256]{1,2,0:T(8,128)S(1)}, f32[2,2,256]{1,2,0:T(8,128)S(1)}, u32[]{:S(2)}, u32[]{:S(2)}) %collective-permute-start.5) | collective-permute-done | bytes 4128 | tf_op jit(solution)/shard_map/ppermute | solution.py:17
  308.2 0.1 pad_maximum_fusion.7
  308.3 4.4 %collective-permute-start.6 = (f32[2,516,2]{1,2,0:T(2,128)S(1)}, f32[2,516,2]{1,2,0:T(2,128)S(1)}, u32[]{:S(2)}, u32[]{:S(2)}) collective-permute-start(f32[2,516,2]{1,2,0:T(2,128)S(1)} %get-tuple-element.9), channel_id=1, source_target_pairs={{0,1},{1,2},{2,3},{3,4},{4,5},{5,6},{6,7},{7,8},{8,9},{9,10},{10,1... | collective-permute-start | bytes 24776 | tf_op jit(solution)/shard_map/ppermute | solution.py:15
  312.7 2.1 collective-permute-start.7
  314.9 0.0 collective-permute-done.6
  314.9 2.8 collective-permute-done.7
  317.7 2.1 fusion.46
  319.9 2.2 fusion.44
  322.1 2.3 add_add_fusion
  324.4 1.7 fusion.41
  326.0 0.0 copy-start
  326.1 0.0 copy-start.1
  326.1 1.7 fusion.42
  327.8 0.5 copy-done
  328.2 0.7 copy-done.1
  328.9 4.6 %multiply_add_fusion = f32[2,1024,512]{2,1,0:T(8,128)} fusion(f32[2,1024,512]{2,1,0:T(8,128)S(1)} %copy-done, f32[2,1024,512]{2,1,0:T(8,128)S(1)} %fusion.41, f32[2,1024,512]{2,1,0:T(8,128)S(1)} %fusion.42, f32[1024,512]{1,0:T(8,128)S(1)} %copy-done.1, f32[2,260,1024]{2,1,0:T(8,128)S(1)} %add_add_fusion, f32[512]{0:T(512)S(1)} %multiply_add_fusion.4, ...), kind=kOutput, calls=%fused_computation.10 | convolution fusion | flops 554512384 | bytes 21007376 | tf_op jit(solution)/shard_map/rpj,jq->rpq/dot_general | solution.py:57
  (7 shorter events, 0.1 us)
Async XLA Ops:
  6.5 148.8 %all-gather.3.cloned.1.call-start = ((), (), s32[]{:S(2)}) async-start(), calls=%async_computation | async-start | bytes 17825792 | tf_op jit(solution)/shard_map/all_gather | solution.py:74
  7.5 15.0 %collective-permute-start = (f32[2,4,512]{1,2,0:T(8,128)S(1)}, f32[2,4,512]{1,2,0:T(8,128)S(1)}, u32[]{:S(2)}, u32[]{:S(2)}) collective-permute-start(f32[2,4,512]{1,2,0:T(8,128)S(1)} %copy.5), channel_id=1, source_target_pairs={{0,16},{16,32},{32,48},{48,64},{64,80},{80,96},{96,112},{1,17},{17... | collective-permute-start | bytes 49160 | tf_op jit(solution)/shard_map/ppermute | solution.py:15
  12.2 14.7 %collective-permute-start.1 = (f32[2,4,512]{1,2,0:T(8,128)S(1)}, f32[2,4,512]{1,2,0:T(8,128)S(1)}, u32[]{:S(2)}, u32[]{:S(2)}) collective-permute-start(f32[2,4,512]{1,2,0:T(8,128)S(1)} %copy.6), channel_id=1, source_target_pairs={{16,0},{32,16},{48,32},{64,48},{80,64},{96,80},{112,96},{17,1},{33... | collective-permute-start | bytes 49160 | tf_op jit(solution)/shard_map/ppermute | solution.py:17
  34.2 6.8 %collective-permute-start.2 = (f32[2,1032,4]{1,2,0:T(4,128)S(1)}, f32[2,1032,4]{1,2,0:T(4,128)S(1)}, u32[]{:S(2)}, u32[]{:S(2)}) collective-permute-start(f32[2,1032,4]{1,2,0:T(4,128)S(1)} %get-tuple-element.5), channel_id=1, source_target_pairs={{0,1},{1,2},{2,3},{3,4},{4,5},{5,6},{6,7},{7,8},{8,9},{9,10},{10,1... | collective-permute-start | bytes 99080 | tf_op jit(solution)/shard_map/ppermute | solution.py:15
  39.0 5.3 %collective-permute-start.3 = (f32[2,1032,4]{1,2,0:T(4,128)S(1)}, f32[2,1032,4]{1,2,0:T(4,128)S(1)}, u32[]{:S(2)}, u32[]{:S(2)}) collective-permute-start(f32[2,1032,4]{1,2,0:T(4,128)S(1)} %get-tuple-element.6), channel_id=1, source_target_pairs={{1,0},{2,1},{3,2},{4,3},{5,4},{6,5},{7,6},{8,7},{9,8},{10,9},{11,1... | collective-permute-start | bytes 99080 | tf_op jit(solution)/shard_map/ppermute | solution.py:17
  40.9 7.3 %slice-start = ((s8[4718592]{0:T(1024)(128)(4,1)}), s8[4194304]{0:T(1024)(128)(4,1)S(1)}, s32[]{:S(2)}) async-start(s8[4718592]{0:T(1024)(128)(4,1)} %bitcast.44), calls=%async_computation.2 | async-start | bytes 8388608
  40.9 7.3 %slice-start.1 = ((s8[4718592]{0:T(1024)(128)(4,1)}), s8[524288]{0:T(1024)(128)(4,1)S(1)}, s32[]{:S(2)}) async-start(s8[4718592]{0:T(1024)(128)(4,1)} %bitcast.44), calls=%async_computation.3 | async-start | bytes 1048576
  59.2 222.2 %all-gather.5.cloned.1.call-start = ((), (), s32[]{:S(2)}) async-start(), calls=%async_computation.1 | async-start | bytes 9437184 | tf_op jit(solution)/shard_map/all_gather | solution.py:77
  298.1 6.3 %collective-permute-start.4 = (f32[2,2,256]{1,2,0:T(8,128)S(1)}, f32[2,2,256]{1,2,0:T(8,128)S(1)}, u32[]{:S(2)}, u32[]{:S(2)}) collective-permute-start(f32[2,2,256]{1,2,0:T(8,128)S(1)} %get-tuple-element.11), channel_id=1, source_target_pairs={{0,16},{16,32},{32,48},{48,64},{64,80},{80,96},{96,112},{1,17},{17... | collective-permute-start | bytes 12296 | tf_op jit(solution)/shard_map/ppermute | solution.py:15
  299.9 8.3 %collective-permute-start.5 = (f32[2,2,256]{1,2,0:T(8,128)S(1)}, f32[2,2,256]{1,2,0:T(8,128)S(1)}, u32[]{:S(2)}, u32[]{:S(2)}) collective-permute-start(f32[2,2,256]{1,2,0:T(8,128)S(1)} %get-tuple-element.12), channel_id=1, source_target_pairs={{16,0},{32,16},{48,32},{64,48},{80,64},{96,80},{112,96},{17,1},{33... | collective-permute-start | bytes 12296 | tf_op jit(solution)/shard_map/ppermute | solution.py:17
  308.3 6.6 %collective-permute-start.6 = (f32[2,516,2]{1,2,0:T(2,128)S(1)}, f32[2,516,2]{1,2,0:T(2,128)S(1)}, u32[]{:S(2)}, u32[]{:S(2)}) collective-permute-start(f32[2,516,2]{1,2,0:T(2,128)S(1)} %get-tuple-element.9), channel_id=1, source_target_pairs={{0,1},{1,2},{2,3},{3,4},{4,5},{5,6},{6,7},{7,8},{8,9},{9,10},{10,1... | collective-permute-start | bytes 24776 | tf_op jit(solution)/shard_map/ppermute | solution.py:15
  312.7 5.0 %collective-permute-start.7 = (f32[2,516,2]{1,2,0:T(2,128)S(1)}, f32[2,516,2]{1,2,0:T(2,128)S(1)}, u32[]{:S(2)}, u32[]{:S(2)}) collective-permute-start(f32[2,516,2]{1,2,0:T(2,128)S(1)} %get-tuple-element.10), channel_id=1, source_target_pairs={{1,0},{2,1},{3,2},{4,3},{5,4},{6,5},{7,6},{8,7},{9,8},{10,9},{11,1... | collective-permute-start | bytes 24776 | tf_op jit(solution)/shard_map/ppermute | solution.py:17
  326.0 2.2 copy-start
  326.1 2.9 copy-start.1
Sparse Core Ops, SparseCore 0:
  59.3 95.9 all-gather.2
  174.2 107.2 all-gather.4

commit v2 on v1

--- a/solution.py
+++ b/solution.py
@@ -61,25 +61,36 @@
     return total
 
 
+def windows(kernel, starts, width):
+    padded = jnp.pad(kernel, ((0, 0), (2, 2)))
+    return jnp.concatenate([padded[:, start : start + width] for start in starts], axis=1)
+
+
 def body(observed, noise_var, row_kernel, col_kernel):
     highest = lax.Precision.HIGHEST
     tile_rows = row_kernel.shape[0]
     tile_cols = col_kernel.shape[0]
-    extended = with_halo(observed, (("gx", 1), ("gy", 2)), 4)
-    col_adj = tap_table(2 * tile_cols + 8, tile_cols, False, 4)
-    row_adj = tap_table(tile_rows, 2 * tile_rows + 8, True, 4)
-    colsum = exact_dot("rpq,qj->rpj", extended, col_adj, True)
+    ext_rows = tile_rows + 4
+    ext_cols = tile_cols + 4
+    row_count = lax.axis_size("gx")
+    col_count = lax.axis_size("gy")
+    col_rows = with_halo(col_kernel, (("gy", 0),), 2)
+    row_rows = with_halo(row_kernel, (("gx", 0),), 2)
+    col_big = windows(col_rows, [tile_cols * c for c in range(col_count)], ext_cols)
+    row_big = windows(row_rows, [tile_rows * c for c in range(row_count)], ext_rows)
+    col_adj = tap_table(2 * tile_cols, ext_cols, False, 2)
+    row_adj = tap_table(ext_rows, 2 * tile_rows, True, 2)
+    colsum = exact_dot("rpq,qj->rpj", observed, col_adj, True)
     inducing = exact_dot("ip,rpj->rij", colsum, row_adj, False)
     mixed = jnp.einsum(
-        "rik,jk->rij", lax.all_gather(inducing, "gy", axis=2, tiled=True), col_kernel, precision=highest
+        "rik,jk->rij", lax.all_gather(inducing, "gy", axis=2, tiled=True), col_big, precision=highest
     )
     product = jnp.einsum(
-        "ik,rkj->rij", row_kernel, lax.all_gather(mixed, "gx", axis=1, tiled=True), precision=highest
+        "ik,rkj->rij", row_big, lax.all_gather(mixed, "gx", axis=1, tiled=True), precision=highest
     )
-    coarse_ext = with_halo(product, (("gx", 1), ("gy", 2)), 2)
-    row_fwd = tap_table(2 * tile_rows, tile_rows + 4, False, 2)
-    col_fwd = tap_table(tile_cols + 4, 2 * tile_cols, True, 2)
-    rowpass = exact_dot("pi,rij->rpj", coarse_ext, row_fwd, False)
+    row_fwd = tap_table(2 * tile_rows, ext_rows, False, 2)
+    col_fwd = tap_table(ext_cols, 2 * tile_cols, True, 2)
+    rowpass = exact_dot("pi,rij->rpj", product, row_fwd, False)
     result = exact_dot("rpj,jq->rpq", rowpass, col_fwd, True)
     return result + noise_var[None] * observed
 

time: 344 us -> 418 us (1.22); the launches traced: 340 us -> 410 us
  matrix products: 64.6 us -> 127 us
  local copies, waits for them, and re-layouts: 15.2 us -> 33.3 us
  waiting for transfers between devices: 224 us -> 213 us
  starting transfers between devices: 22.2 us -> 11.3 us
  other arithmetic: 0.15 us -> 10.5 us
    dot_general x1, matrix products: 16.5 us -> 78.3 us  [body(): jnp.einsum('ik,rkj->rij', row_big, lax.all_gather(mixed, 'gx', axis=1, ti...]
    concatenate x1 -> x2, local copies, waits for them, and re-layouts: 6.38 us -> 18.1 us  [windows(): jnp.concatenate([padded[:, start:start + width] for start in starts], axi...]
    slice x2, local copies, waits for them, and re-layouts: 1 us -> 9.73 us  [windows(): padded[:, start:start + width]]
    concatenate x0 -> x2, other arithmetic: none -> 8.08 us  [with_halo(): jnp.concatenate([lax.ppermute(tail, axis, [(i, (i + 1) % count) for i in...]
    ppermute x4 -> x2, waiting for transfers between devices: 14.4 us -> 6.39 us  [with_halo(): lax.ppermute(head, axis, [((i + 1) % count, i) for i in range(ends)])]
    ppermute x4 -> x2, starting transfers between devices: 15.4 us -> 7.77 us  [with_halo(): lax.ppermute(tail, axis, [(i, (i + 1) % count) for i in range(ends)])]
    ppermute x4 -> x2, waiting for transfers between devices: 6.81 us -> 0.01 us  [with_halo(): lax.ppermute(tail, axis, [(i, (i + 1) % count) for i in range(ends)])]
    all_gather x1, waiting for transfers between devices: 107 us -> 114 us  [body(): lax.all_gather(mixed, 'gx', axis=1, tiled=True)]
  transfers between devices with their start and end apart: 10 -> 6, of which waited for: 8 -> 4; matrix products, arithmetic and copies ran while one was open for 2% -> 9% of each run, Pallas kernels for 0% -> 0%
where the time goes in v2:
time: 418 us; the launch traced here: 410 us
  waiting for transfers between devices  213 us (51%)
  matrix products  127 us (30%)
  local copies, waits for them, and re-layouts  33.3 us (8%)
  between operations  14 us (3%)
  starting transfers between devices  11.3 us (3%)
  other arithmetic  10.5 us (3%)
    all_gather x1, waiting for transfers between devices, body(): lax.all_gather(mixed, 'gx', axis=1, tiled=True)  114 us
    all_gather x1, waiting for transfers between devices, body(): lax.all_gather(inducing, 'gy', axis=2, tiled=True)  93.2 us
    dot_general x1, matrix products, body(): jnp.einsum('ik,rkj->rij', row_big, lax.all_gather(mixed, 'gx', axis=1, ti...  78.3 us
    dot_general x1, matrix products, body(): jnp.einsum('rik,jk->rij', lax.all_gather(inducing, 'gy', axis=2, tiled=Tr...  24.1 us
    concatenate x2, local copies, waits for them, and re-layouts, windows(): jnp.concatenate([padded[:, start:start + width] for start in starts], axi...  18.1 us
    dot_general x6, matrix products, exact_dot(): term = jnp.einsum(eq, part, table, preferred_element_type=jnp.float32)  13.6 us
    dot_general x6, matrix products, exact_dot(): term = jnp.einsum(eq, table, part, preferred_element_type=jnp.float32)  11.3 us
    slice x2, local copies, waits for them, and re-layouts, windows(): padded[:, start:start + width]  9.73 us
  transfers between devices with their start and end apart: 6, of which 4 were waited for; matrix products, arithmetic and copies ran while one was open for 9% of the time, Pallas kernels for 0%

profile of v2, /device:TPU:1, one launch (start us, length us, event | category | flops | bytes accessed | tf_op | source)
XLA Modules:
  0.0 409.9 jit_solution(3492764134755525815)
XLA Ops:
  6.5 0.0 all-gather.3.cloned.1.call-start
  6.6 0.0 copy-start
  6.6 3.5 fusion.20
  10.1 0.0 copy-done
  10.1 1.0 fusion.23
  11.2 1.1 fusion.9
  12.3 1.9 fusion.32
  14.2 1.7 fusion.34
  16.0 1.8 fusion.35
  17.8 2.4 fusion.30
  20.2 0.0 all-gather.3.cloned.1.call-update
  20.3 0.0 all-gather.5.cloned.1.call-start
  20.3 1.0 fusion.200
  21.3 4.6 %collective-permute-start = (f32[2,4096]{1,0:T(2,128)S(1)}, f32[2,4096]{1,0:T(2,128)S(1)}, u32[]{:S(2)}, u32[]{:S(2)}) collective-permute-start(f32[2,4096]{1,0:T(2,128)S(1)} %get-tuple-element.31), channel_id=1, source_target_pairs={{0,1},{1,2},{2,3},{3,4},{4,5},{5,6},{6,7},{7,8},{8,9},{9,10},{10,1... | collective-permute-start | bytes 98312 | tf_op jit(solution)/shard_map/ppermute | solution.py:15
  25.9 2.2 collective-permute-start.1
  28.1 0.0 collective-permute-done
  28.1 3.0 collective-permute-done.1
  31.1 2.9 pad_maximum_fusion.1
  34.0 3.4 pad_slice_fusion.2
  37.4 6.3 %concatenate.13 = f32[260,4160]{1,0:T(8,128)} concatenate(f32[260,260]{1,0:T(8,128)} %get-tuple-element.30, f32[260,260]{1,0:T(8,128)} %get-tuple-element.29, f32[260,260]{1,0:T(8,128)} %get-tuple-element.28, f32[260,260]{1,0:T(8,128)} %get-tuple-element.27, f32[260,260]{1,0:T(8,128)} %get-tuple-element.26, f32[260,260]{1,0:T(8,128)} %get-tuple-element.25, ...), dimensions={1} | concatenate | bytes 8652800 | tf_op jit(solution)/shard_map/concatenate | solution.py:66
  43.7 93.2 %all-gather.3.cloned.1.call-done = f32[2,516,4160]{1,0,2:T(2,128)} async-done(((f32[2,516,260]{1,0,2:T(2,128)}), f32[2,516,4160]{1,0,2:T(2,128)}) %all-gather.3.cloned.1.call-update) | async-done | bytes 17172496 | tf_op jit(solution)/shard_map/all_gather | solution.py:86
  136.9 24.1 %fusion = f32[2,516,260]{1,2,0:T(8,128)S(1)} fusion(f32[2,516,4160]{1,0,2:T(2,128)} %all-gather.3.cloned.1.call-done, f32[260,4160]{1,0:T(8,128)} %concatenate.13), kind=kOutput, calls=%fused_computation | convolution fusion | flops 13394534400 | bytes 22572160 | tf_op jit(solution)/shard_map/rik,jk->rij/dot_general | solution.py:85
  161.1 2.2 copy.10
  163.3 0.0 all-gather.5.cloned.1.call-update
  163.3 1.0 fusion.199
  164.3 3.2 collective-permute-start.2
  167.5 1.3 collective-permute-start.3
  168.8 0.0 collective-permute-done.2
  168.8 3.3 collective-permute-done.3
  172.2 5.2 %pad_maximum_fusion = f32[516,4096]{1,0:T(8,128)S(1)} fusion(f32[2,4096]{1,0:T(2,128)S(1)} %collective-permute-done.3, f32[512,4096]{1,0:T(8,128)} %param.6, f32[2,4096]{1,0:T(2,128)S(1)} %collective-permute-done.2), kind=kLoop, calls=%fused_computation.5 | loop fusion | flops 4227072 | bytes 16908288 | tf_op jit(solution)/shard_map/concatenate | solution.py:13
  177.3 6.4 %pad_slice_fusion = (f32[516,516]{1,0:T(8,128)S(1)}, f32[516,516]{1,0:T(8,128)}, f32[516,516]{1,0:T(8,128)}, f32[516,516]{1,0:T(8,128)}, f32[516,516]{1,0:T(8,12...) fusion(f32[516,4096]{1,0:T(8,128)S(1)} %pad_maximum_fusion), kind=kLoop, calls=%fused_computation.6 | loop fusion | bytes 25027072 | tf_op jit(solution)/shard_map/slice | solution.py:66
  183.7 11.8 %concatenate.15 = f32[516,4128]{1,0:T(8,128)} concatenate(f32[516,516]{1,0:T(8,128)} %get-tuple-element.12, f32[516,516]{1,0:T(8,128)} %get-tuple-element.11, f32[516,516]{1,0:T(8,128)} %get-tuple-element.10, f32[516,516]{1,0:T(8,128)} %get-tuple-element.9, f32[516,516]{1,0:T(8,128)} %get-tuple-element.8, f32[516,516]{1,0:T(8,128)} %get-tuple-element.7, ...), dimensions={1} | concatenate | bytes 17040384 | tf_op jit(solution)/shard_map/concatenate | solution.py:66
  195.5 113.9 %all-gather.5.cloned.1.call-done = f32[2,4128,260]{2,0,1:T(2,128)} async-done(((f32[2,516,260]{2,0,1:T(2,128)}), f32[2,4128,260]{2,0,1:T(2,128)}) %all-gather.5.cloned.1.call-update) | async-done | bytes 8586256 | tf_op jit(solution)/shard_map/all_gather | solution.py:89
  309.4 78.3 %fusion.24 = f32[2,516,260]{1,2,0:T(8,128)S(1)} fusion(f32[516,4128]{1,0:T(8,128)} %concatenate.15, f32[2,4128,260]{2,0,1:T(2,128)} %all-gather.5.cloned.1.call-done), kind=kOutput, calls=%fused_computation.52 | convolution fusion | flops 13291499520 | bytes 18179712 | tf_op jit(solution)/shard_map/ik,rkj->rij/dot_general | solution.py:88
  387.7 1.9 fusion.41
  389.6 1.8 fusion.43
  391.4 2.1 add_add_fusion
  393.5 1.7 fusion.37
  395.2 0.0 copy-start.1
  395.2 0.0 copy-start.2
  395.2 1.7 fusion.36
  396.9 0.5 copy-done.1
  397.4 0.7 copy-done.2
  398.1 4.6 %multiply_add_fusion = f32[2,1024,512]{2,1,0:T(8,128)} fusion(f32[2,1024,512]{2,1,0:T(8,128)S(1)} %copy-done.1, f32[2,1024,512]{2,1,0:T(8,128)S(1)} %fusion.36, f32[2,1024,512]{2,1,0:T(8,128)S(1)} %fusion.37, f32[1024,512]{1,0:T(8,128)S(1)} %copy-done.2, f32[2,260,1024]{2,1,0:T(8,128)S(1)} %add_add_fusion, f32[512]{0:T(512)S(1)} %multiply_add_fusion.2, ...), kind=kOutput, calls=%fused_computation.17 | convolution fusion | flops 554512384 | bytes 21007376 | tf_op jit(solution)/shard_map/rpj,jq->rpq/dot_general | solution.py:57
  (4 shorter events, 0.0 us)
Async XLA Ops:
  6.5 130.4 %all-gather.3.cloned.1.call-start = ((), (), s32[]{:S(2)}) async-start(), calls=%async_computation | async-start | bytes 22630400 | tf_op jit(solution)/shard_map/all_gather | solution.py:86
  6.6 3.5 copy-start
  20.3 289.1 %all-gather.5.cloned.1.call-start = ((), (), s32[]{:S(2)}) async-start(), calls=%async_computation.1 | async-start | bytes 14266368 | tf_op jit(solution)/shard_map/all_gather | solution.py:89
  21.3 6.8 %collective-permute-start = (f32[2,4096]{1,0:T(2,128)S(1)}, f32[2,4096]{1,0:T(2,128)S(1)}, u32[]{:S(2)}, u32[]{:S(2)}) collective-permute-start(f32[2,4096]{1,0:T(2,128)S(1)} %get-tuple-element.31), channel_id=1, source_target_pairs={{0,1},{1,2},{2,3},{3,4},{4,5},{5,6},{6,7},{7,8},{8,9},{9,10},{10,1... | collective-permute-start | bytes 98312 | tf_op jit(solution)/shard_map/ppermute | solution.py:15
  25.9 5.2 %collective-permute-start.1 = (f32[2,4096]{1,0:T(2,128)S(1)}, f32[2,4096]{1,0:T(2,128)S(1)}, u32[]{:S(2)}, u32[]{:S(2)}) collective-permute-start(f32[2,4096]{1,0:T(2,128)S(1)} %get-tuple-element.32), channel_id=1, source_target_pairs={{1,0},{2,1},{3,2},{4,3},{5,4},{6,5},{7,6},{8,7},{9,8},{10,9},{11,1... | collective-permute-start | bytes 98312 | tf_op jit(solution)/shard_map/ppermute | solution.py:17
  164.3 4.5 %collective-permute-start.2 = (f32[2,4096]{1,0:T(2,128)S(1)}, f32[2,4096]{1,0:T(2,128)S(1)}, u32[]{:S(2)}, u32[]{:S(2)}) collective-permute-start(f32[2,4096]{1,0:T(2,128)S(1)} %get-tuple-element.13), channel_id=1, source_target_pairs={{0,16},{16,32},{32,48},{48,64},{64,80},{80,96},{96,112},{1,17},{17... | collective-permute-start | bytes 98312 | tf_op jit(solution)/shard_map/ppermute | solution.py:15
  167.5 4.7 %collective-permute-start.3 = (f32[2,4096]{1,0:T(2,128)S(1)}, f32[2,4096]{1,0:T(2,128)S(1)}, u32[]{:S(2)}, u32[]{:S(2)}) collective-permute-start(f32[2,4096]{1,0:T(2,128)S(1)} %get-tuple-element.14), channel_id=1, source_target_pairs={{16,0},{32,16},{48,32},{64,48},{80,64},{96,80},{112,96},{17,1},{33... | collective-permute-start | bytes 98312 | tf_op jit(solution)/shard_map/ppermute | solution.py:17
  395.2 2.2 copy-start.1
  395.2 2.9 copy-start.2
Sparse Core Ops, SparseCore 0:
  20.4 116.5 all-gather.2
  163.4 145.8 all-gather.4

commit v3 on v1

--- a/solution.py
+++ b/solution.py
@@ -61,23 +61,32 @@
     return total
 
 
+def row_windows(kernel, count, block, width):
+    padded = jnp.pad(kernel, ((0, width - kernel.shape[0]), (2, width - block - 2)))
+    return jnp.concatenate([padded[:, block * w : block * w + width] for w in range(count)], axis=1)
+
+
 def body(observed, noise_var, row_kernel, col_kernel):
     highest = lax.Precision.HIGHEST
     tile_rows = row_kernel.shape[0]
     tile_cols = col_kernel.shape[0]
-    extended = with_halo(observed, (("gx", 1), ("gy", 2)), 4)
+    ext_rows = tile_rows + 8
+    row_count = lax.axis_size("gx")
+    row_rows = with_halo(row_kernel, (("gx", 0),), 2)
+    row_big = row_windows(row_rows, row_count, tile_rows, ext_rows)
+    extended = with_halo(observed, (("gy", 2),), 4)
     col_adj = tap_table(2 * tile_cols + 8, tile_cols, False, 4)
-    row_adj = tap_table(tile_rows, 2 * tile_rows + 8, True, 4)
+    row_adj = tap_table(ext_rows, 2 * tile_rows, True, 2)
     colsum = exact_dot("rpq,qj->rpj", extended, col_adj, True)
     inducing = exact_dot("ip,rpj->rij", colsum, row_adj, False)
     mixed = jnp.einsum(
         "rik,jk->rij", lax.all_gather(inducing, "gy", axis=2, tiled=True), col_kernel, precision=highest
     )
     product = jnp.einsum(
-        "ik,rkj->rij", row_kernel, lax.all_gather(mixed, "gx", axis=1, tiled=True), precision=highest
+        "ik,rkj->rij", row_big, lax.all_gather(mixed, "gx", axis=1, tiled=True), precision=highest
     )
-    coarse_ext = with_halo(product, (("gx", 1), ("gy", 2)), 2)
-    row_fwd = tap_table(2 * tile_rows, tile_rows + 4, False, 2)
+    coarse_ext = with_halo(product, (("gy", 2),), 2)
+    row_fwd = tap_table(2 * tile_rows, ext_rows, False, 2)
     col_fwd = tap_table(tile_cols + 4, 2 * tile_cols, True, 2)
     rowpass = exact_dot("pi,rij->rpj", coarse_ext, row_fwd, False)
     result = exact_dot("rpj,jq->rpq", rowpass, col_fwd, True)

time: 344 us -> 321 us (0.933)
  waiting for transfers between devices: 224 us -> 176 us
  other arithmetic: 0.15 us -> 11.1 us
  local copies, waits for them, and re-layouts: 15.2 us -> 24.5 us
    all_gather x1, waiting for transfers between devices: 107 us -> 73.8 us  [body(): lax.all_gather(mixed, 'gx', axis=1, tiled=True)]
    concatenate x0 -> x1, other arithmetic: none -> 11 us  [with_halo(): jnp.concatenate([lax.ppermute(tail, axis, [(i, (i + 1) % count) for i in...]
    ppermute x4 -> x3, waiting for transfers between devices: 14.4 us -> 6.58 us  [with_halo(): lax.ppermute(head, axis, [((i + 1) % count, i) for i in range(ends)])]
    ppermute x4 -> x3, starting transfers between devices: 6.65 us -> 14.1 us  [with_halo(): lax.ppermute(head, axis, [((i + 1) % count, i) for i in range(ends)])]
    ppermute x4 -> x3, waiting for transfers between devices: 6.81 us -> 0.01 us  [with_halo(): lax.ppermute(tail, axis, [(i, (i + 1) % count) for i in range(ends)])]
    concatenate x1, local copies, waits for them, and re-layouts: 6.38 us -> 11.6 us  [row_windows(): jnp.concatenate([padded[:, block * w:block * w + width] for w in range(co...]
    ppermute x4 -> x3, starting transfers between devices: 15.4 us -> 10.9 us  [with_halo(): lax.ppermute(tail, axis, [(i, (i + 1) % count) for i in range(ends)])]
  transfers between devices with their start and end apart: 10 -> 8, of which waited for: 8 -> 4; matrix products, arithmetic and copies ran while one was open for 2% -> 9% of each run, Pallas kernels for 0% -> 0%
where the time goes in v3:
time: 321 us; the launch traced here: 315 us
  waiting for transfers between devices  176 us (55%)
  matrix products  65 us (20%)
  starting transfers between devices  25.3 us (8%)
  local copies, waits for them, and re-layouts  24.5 us (8%)
  between operations  13.8 us (4%)
  other arithmetic  11.1 us (3%)
    all_gather x1, waiting for transfers between devices, body(): lax.all_gather(inducing, 'gy', axis=2, tiled=True)  95.4 us
    all_gather x1, waiting for transfers between devices, body(): lax.all_gather(mixed, 'gx', axis=1, tiled=True)  73.8 us
    dot_general x1, matrix products, body(): jnp.einsum('ik,rkj->rij', row_big, lax.all_gather(mixed, 'gx', axis=1, ti...  18.4 us
    dot_general x1, matrix products, body(): jnp.einsum('rik,jk->rij', lax.all_gather(inducing, 'gy', axis=2, tiled=Tr...  17.6 us
    dot_general x6, matrix products, exact_dot(): term = jnp.einsum(eq, part, table, preferred_element_type=jnp.float32)  15.2 us
    ppermute x3, starting transfers between devices, with_halo(): lax.ppermute(head, axis, [((i + 1) % count, i) for i in range(ends)])  14.1 us
    dot_general x6, matrix products, exact_dot(): term = jnp.einsum(eq, table, part, preferred_element_type=jnp.float32)  13.7 us
    concatenate x1, local copies, waits for them, and re-layouts, row_windows(): jnp.concatenate([padded[:, block * w:block * w + width] for w in range(co...  11.6 us
  transfers between devices with their start and end apart: 8, of which 4 were waited for; matrix products, arithmetic and copies ran while one was open for 9% of the time, Pallas kernels for 0%

profile of v3, /device:TPU:1, one launch (start us, length us, event | category | flops | bytes accessed | tf_op | source)
XLA Modules:
  0.0 315.5 jit_solution(17095877267252233875)
XLA Ops:
  6.5 0.0 all-gather.3.cloned.1.call-start
  6.5 5.3 %copy.21 = f32[2,1024,512]{1,2,0:T(8,128)} copy(f32[2,1024,512]{2,1,0:T(8,128)} %param.4) | data formatting | bytes 8388608 | tf_op args[0]
  11.9 0.9 fusion.204
  12.8 4.6 %collective-permute-start = (f32[2,1024,4]{1,2,0:T(4,128)S(1)}, f32[2,1024,4]{1,2,0:T(4,128)S(1)}, u32[]{:S(2)}, u32[]{:S(2)}) collective-permute-start(f32[2,1024,4]{1,2,0:T(4,128)S(1)} %get-tuple-element.15), channel_id=1, source_target_pairs={{0,1},{1,2},{2,3},{3,4},{4,5},{5,6},{6,7},{7,8},{8,9},{9,10},{10,1... | collective-permute-start | bytes 98312 | tf_op jit(solution)/shard_map/ppermute | solution.py:15
  17.4 1.9 collective-permute-start.1
  19.3 0.0 copy-start.2
  19.4 0.0 collective-permute-done
  19.4 3.2 %collective-permute-done.1 = f32[2,1024,4]{1,2,0:T(4,128)S(1)} collective-permute-done((f32[2,1024,4]{1,2,0:T(4,128)S(1)}, f32[2,1024,4]{1,2,0:T(4,128)S(1)}, u32[]{:S(2)}, u32[]{:S(2)}) %collective-permute-start.1) | collective-permute-done | bytes 32800 | tf_op jit(solution)/shard_map/ppermute | solution.py:17
  22.6 3.8 %fusion.17 = f32[2,1024,256]{2,1,0:T(8,128)S(1)} fusion(f32[2,1024,4]{1,2,0:T(4,128)S(1)} %collective-permute-done.1, f32[2,1024,512]{1,2,0:T(8,128)} %copy.21, f32[2,1024,4]{1,2,0:T(4,128)S(1)} %collective-permute-done, f32[520]{0:T(1024)S(1)} %multiply_add_fusion.2), kind=kOutput, calls=%fused_computation.42 | convolution fusion | flops 554045440 | bytes 6359072 | tf_op jit(solution)/shard_map/rpq,qj->rpj/dot_general | solution.py:57
  26.4 0.0 copy-done.2
  26.4 1.6 fusion.16
  28.0 2.0 add_add_fusion.1
  30.0 1.4 fusion.51
  31.3 1.5 convolution_add_fusion.1
  32.8 2.6 fusion.29
  35.4 0.0 all-gather.3.cloned.1.call-update
  35.5 0.3 all-gather.5.cloned.1.call-start
  35.8 95.4 %all-gather.3.cloned.1.call-done = f32[2,520,4096]{2,1,0:T(8,128)} async-done(((f32[2,520,256]{2,1,0:T(8,128)}), f32[2,520,4096]{2,1,0:T(8,128)}) %all-gather.3.cloned.1.call-update) | async-done | bytes 17039376 | tf_op jit(solution)/shard_map/all_gather | solution.py:83
  131.2 17.6 %fusion.5 = f32[2,520,256]{2,1,0:T(8,128)} fusion(f32[2,520,4096]{2,1,0:T(8,128)} %all-gather.3.cloned.1.call-done, f32[256,4096]{1,0:T(8,128)} %param.7), kind=kOutput, calls=%fused_computation.15 | convolution fusion | flops 13086228480 | bytes 22298624 | tf_op jit(solution)/shard_map/rik,jk->rij/dot_general | solution.py:82
  148.8 0.0 all-gather.5.cloned.1.call-update
  148.8 1.0 fusion.203
  149.8 3.2 %collective-permute-start.2 = (f32[2,4096]{1,0:T(2,128)S(1)}, f32[2,4096]{1,0:T(2,128)S(1)}, u32[]{:S(2)}, u32[]{:S(2)}) collective-permute-start(f32[2,4096]{1,0:T(2,128)S(1)} %get-tuple-element.13), channel_id=1, source_target_pairs={{0,16},{16,32},{32,48},{48,64},{64,80},{80,96},{96,112},{1,17},{17... | collective-permute-start | bytes 98312 | tf_op jit(solution)/shard_map/ppermute | solution.py:15
  153.0 1.3 collective-permute-start.3
  154.3 0.0 collective-permute-done.2
  154.3 3.3 %collective-permute-done.3 = f32[2,4096]{1,0:T(2,128)S(1)} collective-permute-done((f32[2,4096]{1,0:T(2,128)S(1)}, f32[2,4096]{1,0:T(2,128)S(1)}, u32[]{:S(2)}, u32[]{:S(2)}) %collective-permute-start.3) | collective-permute-done | bytes 32800 | tf_op jit(solution)/shard_map/ppermute | solution.py:17
  157.7 11.0 %select_maximum_fusion = f32[520,4104]{1,0:T(8,128)S(1)} fusion(f32[2,4096]{1,0:T(2,128)S(1)} %collective-permute-done.3, f32[512,4096]{1,0:T(8,128)} %param.6, f32[2,4096]{1,0:T(2,128)S(1)} %collective-permute-done.2), kind=kLoop, calls=%fused_computation.2 | loop fusion | flops 27743040 | bytes 16990464 | tf_op jit(solution)/shard_map/concatenate | solution.py:13
  168.7 3.3 %fusion.202 = (f32[520,520]{1,0:T(8,128)S(1)}, f32[520,520]{1,0:T(8,128)S(1)}, f32[520,520]{1,0:T(8,128)}, f32[520,520]{1,0:T(8,128)}, f32[520,520]{1,0:T(8,128)...) fusion(f32[520,4104]{1,0:T(8,128)S(1)} %select_maximum_fusion), kind=kLoop, calls=%fused_computation.223 | loop fusion | bytes 17305600 | tf_op jit(solution)/shard_map/slice | solution.py:66
  172.1 11.6 %concatenate.14 = f32[520,4160]{1,0:T(8,128)} concatenate(f32[520,520]{1,0:T(8,128)} %get-tuple-element.12, f32[520,520]{1,0:T(8,128)} %get-tuple-element.11, f32[520,520]{1,0:T(8,128)} %get-tuple-element.10, f32[520,520]{1,0:T(8,128)} %get-tuple-element.9, f32[520,520]{1,0:T(8,128)} %get-tuple-element.8, f32[520,520]{1,0:T(8,128)} %get-tuple-element.7, ...), dimensions={1} | concatenate | bytes 17305600 | tf_op jit(solution)/shard_map/concatenate | solution.py:66
  183.7 73.8 %all-gather.5.cloned.1.call-done = f32[2,4160,256]{2,1,0:T(8,128)} async-done(((f32[2,520,256]{2,1,0:T(8,128)}), f32[2,4160,256]{2,1,0:T(8,128)}) %all-gather.5.cloned.1.call-update) | async-done | bytes 8519696 | tf_op jit(solution)/shard_map/all_gather | solution.py:86
  257.4 18.4 %fusion.26 = f32[2,520,256]{2,1,0:T(8,128)S(1)} fusion(f32[2,4160,256]{2,1,0:T(8,128)} %all-gather.5.cloned.1.call-done, f32[520,4160]{1,0:T(8,128)} %concatenate.14), kind=kOutput, calls=%fused_computation.53 | convolution fusion | flops 13290700800 | bytes 18237440 | tf_op jit(solution)/shard_map/ik,rkj->rij/dot_general | solution.py:85
  275.9 0.2 fusion.205
  276.1 0.2 copy.24
  276.3 3.2 %collective-permute-start.4 = (f32[2,520,2]{1,2,0:T(2,128)S(1)}, f32[2,520,2]{1,2,0:T(2,128)S(1)}, u32[]{:S(2)}, u32[]{:S(2)}) collective-permute-start(f32[2,520,2]{1,2,0:T(2,128)S(1)} %copy.24), channel_id=1, source_target_pairs={{0,1},{1,2},{2,3},{3,4},{4,5},{5,6},{6,7},{7,8},{8,9},{9,10},{10,1... | collective-permute-start | bytes 24968 | tf_op jit(solution)/shard_map/ppermute | solution.py:15
  279.5 0.2 copy.25
  279.7 10.8 %collective-permute-start.5 = (f32[2,520,2]{1,2,0:T(2,128)S(1)}, f32[2,520,2]{1,2,0:T(2,128)S(1)}, u32[]{:S(2)}, u32[]{:S(2)}) collective-permute-start(f32[2,520,2]{1,2,0:T(2,128)S(1)} %copy.25), channel_id=1, source_target_pairs={{1,0},{2,1},{3,2},{4,3},{5,4},{6,5},{7,6},{8,7},{9,8},{10,9},{11,1... | collective-permute-start | bytes 24968 | tf_op jit(solution)/shard_map/ppermute | solution.py:17
  290.6 0.0 collective-permute-done.4
  290.6 0.2 copy.26
  290.8 0.0 collective-permute-done.5
  290.8 0.2 copy.27
  291.1 2.8 fusion.37
  293.9 2.9 fusion.35
  296.7 2.6 add_add_fusion
  299.3 1.7 fusion.31
  301.0 0.0 copy-start
  301.0 0.0 copy-start.1
  301.0 1.7 fusion.32
  302.7 0.5 copy-done
  303.2 0.7 copy-done.1
  303.9 4.6 %multiply_add_fusion = f32[2,1024,512]{2,1,0:T(8,128)} fusion(f32[2,1024,512]{2,1,0:T(8,128)S(1)} %copy-done, f32[2,1024,512]{2,1,0:T(8,128)S(1)} %fusion.31, f32[2,1024,512]{2,1,0:T(8,128)S(1)} %fusion.32, f32[1024,512]{1,0:T(8,128)S(1)} %copy-done.1, f32[2,260,1024]{2,1,0:T(8,128)S(1)} %add_add_fusion, f32[512]{0:T(512)S(1)} %multiply_add_fusion.3, ...), kind=kOutput, calls=%fused_computation.17 | convolution fusion | flops 554512384 | bytes 21007376 | tf_op jit(solution)/shard_map/rpj,jq->rpq/dot_general | solution.py:57
  (5 shorter events, 0.0 us)
Async XLA Ops:
  6.5 124.7 %all-gather.3.cloned.1.call-start = ((), (), s32[]{:S(2)}) async-start(), calls=%async_computation | async-start | bytes 18104320 | tf_op jit(solution)/shard_map/all_gather | solution.py:83
  12.8 6.6 %collective-permute-start = (f32[2,1024,4]{1,2,0:T(4,128)S(1)}, f32[2,1024,4]{1,2,0:T(4,128)S(1)}, u32[]{:S(2)}, u32[]{:S(2)}) collective-permute-start(f32[2,1024,4]{1,2,0:T(4,128)S(1)} %get-tuple-element.15), channel_id=1, source_target_pairs={{0,1},{1,2},{2,3},{3,4},{4,5},{5,6},{6,7},{7,8},{8,9},{9,10},{10,1... | collective-permute-start | bytes 98312 | tf_op jit(solution)/shard_map/ppermute | solution.py:15
  17.4 5.2 %collective-permute-start.1 = (f32[2,1024,4]{1,2,0:T(4,128)S(1)}, f32[2,1024,4]{1,2,0:T(4,128)S(1)}, u32[]{:S(2)}, u32[]{:S(2)}) collective-permute-start(f32[2,1024,4]{1,2,0:T(4,128)S(1)} %get-tuple-element.16), channel_id=1, source_target_pairs={{1,0},{2,1},{3,2},{4,3},{5,4},{6,5},{7,6},{8,7},{9,8},{10,9},{11,1... | collective-permute-start | bytes 98312 | tf_op jit(solution)/shard_map/ppermute | solution.py:17
  19.3 7.1 %copy-start.2 = (f32[2,1024,512]{1,2,0:T(8,128)S(1)}, f32[2,1024,512]{1,2,0:T(8,128)}, u32[]{:S(2)}) copy-start(f32[2,1024,512]{1,2,0:T(8,128)} %copy.21) | copy-start | bytes 12582916
  35.5 222.0 %all-gather.5.cloned.1.call-start = ((), (), s32[]{:S(2)}) async-start(), calls=%async_computation.1 | async-start | bytes 9584640 | tf_op jit(solution)/shard_map/all_gather | solution.py:86
  149.8 4.5 %collective-permute-start.2 = (f32[2,4096]{1,0:T(2,128)S(1)}, f32[2,4096]{1,0:T(2,128)S(1)}, u32[]{:S(2)}, u32[]{:S(2)}) collective-permute-start(f32[2,4096]{1,0:T(2,128)S(1)} %get-tuple-element.13), channel_id=1, source_target_pairs={{0,16},{16,32},{32,48},{48,64},{64,80},{80,96},{96,112},{1,17},{17... | collective-permute-start | bytes 98312 | tf_op jit(solution)/shard_map/ppermute | solution.py:15
  153.0 4.7 %collective-permute-start.3 = (f32[2,4096]{1,0:T(2,128)S(1)}, f32[2,4096]{1,0:T(2,128)S(1)}, u32[]{:S(2)}, u32[]{:S(2)}) collective-permute-start(f32[2,4096]{1,0:T(2,128)S(1)} %get-tuple-element.14), channel_id=1, source_target_pairs={{16,0},{32,16},{48,32},{64,48},{80,64},{96,80},{112,96},{17,1},{33... | collective-permute-start | bytes 98312 | tf_op jit(solution)/shard_map/ppermute | solution.py:17
  276.3 14.3 %collective-permute-start.4 = (f32[2,520,2]{1,2,0:T(2,128)S(1)}, f32[2,520,2]{1,2,0:T(2,128)S(1)}, u32[]{:S(2)}, u32[]{:S(2)}) collective-permute-start(f32[2,520,2]{1,2,0:T(2,128)S(1)} %copy.24), channel_id=1, source_target_pairs={{0,1},{1,2},{2,3},{3,4},{4,5},{5,6},{6,7},{7,8},{8,9},{9,10},{10,1... | collective-permute-start | bytes 24968 | tf_op jit(solution)/shard_map/ppermute | solution.py:15
  279.7 11.1 %collective-permute-start.5 = (f32[2,520,2]{1,2,0:T(2,128)S(1)}, f32[2,520,2]{1,2,0:T(2,128)S(1)}, u32[]{:S(2)}, u32[]{:S(2)}) collective-permute-start(f32[2,520,2]{1,2,0:T(2,128)S(1)} %copy.25), channel_id=1, source_target_pairs={{1,0},{2,1},{3,2},{4,3},{5,4},{6,5},{7,6},{8,7},{9,8},{10,9},{11,1... | collective-permute-start | bytes 24968 | tf_op jit(solution)/shard_map/ppermute | solution.py:17
  301.0 2.2 copy-start
  301.0 2.9 copy-start.1
Sparse Core Ops, SparseCore 0:
  35.6 95.5 all-gather.2
  149.0 108.4 all-gather.4

commit v4 on v3

--- a/solution.py
+++ b/solution.py
@@ -67,7 +67,7 @@
 
 
 def body(observed, noise_var, row_kernel, col_kernel):
-    highest = lax.Precision.HIGHEST
+    highest = lax.Precision.HIGH
     tile_rows = row_kernel.shape[0]
     tile_cols = col_kernel.shape[0]
     ext_rows = tile_rows + 8

time: 321 us -> 299 us (0.931); the launches traced: 315 us -> 298 us
  matrix products: 65 us -> 53.7 us
  starting transfers between devices: 25.3 us -> 16.5 us
    ppermute x3, starting transfers between devices: 14.1 us -> 5.35 us  [with_halo(): lax.ppermute(head, axis, [((i + 1) % count, i) for i in range(ends)])]
    dot_general x1, matrix products: 18.4 us -> 12.2 us  [body(): jnp.einsum('ik,rkj->rij', row_big, lax.all_gather(mixed, 'gx', axis=1, ti...]
    dot_general x1, matrix products: 17.6 us -> 12.5 us  [body(): jnp.einsum('rik,jk->rij', lax.all_gather(inducing, 'gy', axis=2, tiled=Tr...]
  transfers between devices with their start and end apart: 8 -> 8, of which waited for: 4 -> 5; matrix products, arithmetic and copies ran while one was open for 9% -> 9% of each run, Pallas kernels for 0% -> 0%
where the time goes in v4:
time: 299 us; the launch traced here: 298 us
  waiting for transfers between devices  178 us (60%)
  matrix products  53.7 us (18%)
  local copies, waits for them, and re-layouts  24.5 us (8%)
  starting transfers between devices  16.5 us (6%)
  between operations  13.6 us (5%)
  other arithmetic  11.1 us (4%)
    all_gather x1, waiting for transfers between devices, body(): lax.all_gather(inducing, 'gy', axis=2, tiled=True)  95.5 us
    all_gather x1, waiting for transfers between devices, body(): lax.all_gather(mixed, 'gx', axis=1, tiled=True)  73.8 us
    dot_general x6, matrix products, exact_dot(): term = jnp.einsum(eq, part, table, preferred_element_type=jnp.float32)  15.2 us
    dot_general x6, matrix products, exact_dot(): term = jnp.einsum(eq, table, part, preferred_element_type=jnp.float32)  13.7 us
    dot_general x1, matrix products, body(): jnp.einsum('rik,jk->rij', lax.all_gather(inducing, 'gy', axis=2, tiled=Tr...  12.5 us
    dot_general x1, matrix products, body(): jnp.einsum('ik,rkj->rij', row_big, lax.all_gather(mixed, 'gx', axis=1, ti...  12.2 us
    concatenate x1, local copies, waits for them, and re-layouts, row_windows(): jnp.concatenate([padded[:, block * w:block * w + width] for w in range(co...  11.6 us
    concatenate x1, other arithmetic, with_halo(): jnp.concatenate([lax.ppermute(tail, axis, [(i, (i + 1) % count) for i in...  11 us
  transfers between devices with their start and end apart: 8, of which 5 were waited for; matrix products, arithmetic and copies ran while one was open for 9% of the time, Pallas kernels for 0%

profile of v4, /device:TPU:1, one launch (start us, length us, event | category | flops | bytes accessed | tf_op | source)
XLA Modules:
  0.0 297.9 jit_solution(1745938520390472203)
XLA Ops:
  6.5 0.0 all-gather.3.cloned.1.call-start
  6.5 5.3 %copy.21 = f32[2,1024,512]{1,2,0:T(8,128)} copy(f32[2,1024,512]{2,1,0:T(8,128)} %param.4) | data formatting | bytes 8388608 | tf_op args[0]
  11.9 0.9 fusion.204
  12.8 4.6 %collective-permute-start = (f32[2,1024,4]{1,2,0:T(4,128)S(1)}, f32[2,1024,4]{1,2,0:T(4,128)S(1)}, u32[]{:S(2)}, u32[]{:S(2)}) collective-permute-start(f32[2,1024,4]{1,2,0:T(4,128)S(1)} %get-tuple-element.15), channel_id=1, source_target_pairs={{0,1},{1,2},{2,3},{3,4},{4,5},{5,6},{6,7},{7,8},{8,9},{9,10},{10,1... | collective-permute-start | bytes 98312 | tf_op jit(solution)/shard_map/ppermute | solution.py:15
  17.4 1.9 collective-permute-start.1
  19.3 0.0 copy-start.2
  19.4 0.0 collective-permute-done
  19.4 3.2 %collective-permute-done.1 = f32[2,1024,4]{1,2,0:T(4,128)S(1)} collective-permute-done((f32[2,1024,4]{1,2,0:T(4,128)S(1)}, f32[2,1024,4]{1,2,0:T(4,128)S(1)}, u32[]{:S(2)}, u32[]{:S(2)}) %collective-permute-start.1) | collective-permute-done | bytes 32800 | tf_op jit(solution)/shard_map/ppermute | solution.py:17
  22.6 3.8 %fusion.17 = f32[2,1024,256]{2,1,0:T(8,128)S(1)} fusion(f32[2,1024,4]{1,2,0:T(4,128)S(1)} %collective-permute-done.1, f32[2,1024,512]{1,2,0:T(8,128)} %copy.21, f32[2,1024,4]{1,2,0:T(4,128)S(1)} %collective-permute-done, f32[520]{0:T(1024)S(1)} %multiply_add_fusion.2), kind=kOutput, calls=%fused_computation.42 | convolution fusion | flops 554045440 | bytes 6359072 | tf_op jit(solution)/shard_map/rpq,qj->rpj/dot_general | solution.py:57
  26.4 0.0 copy-done.2
  26.4 1.6 fusion.16
  28.0 2.0 add_add_fusion.1
  30.0 1.4 fusion.51
  31.3 1.5 convolution_add_fusion.1
  32.8 2.6 fusion.29
  35.4 0.0 all-gather.3.cloned.1.call-update
  35.5 0.2 all-gather.5.cloned.1.call-start
  35.7 95.5 %all-gather.3.cloned.1.call-done = f32[2,520,4096]{2,1,0:T(8,128)} async-done(((f32[2,520,256]{2,1,0:T(8,128)}), f32[2,520,4096]{2,1,0:T(8,128)}) %all-gather.3.cloned.1.call-update) | async-done | bytes 17039376 | tf_op jit(solution)/shard_map/all_gather | solution.py:83
  131.2 12.5 %fusion.5 = f32[2,520,256]{2,1,0:T(8,128)} fusion(f32[2,520,4096]{2,1,0:T(8,128)} %all-gather.3.cloned.1.call-done, f32[256,4096]{1,0:T(8,128)} %param.7), kind=kOutput, calls=%fused_computation.15 | convolution fusion | flops 6543114240 | bytes 22298624 | tf_op jit(solution)/shard_map/rik,jk->rij/dot_general | solution.py:82
  143.8 0.0 all-gather.5.cloned.1.call-update
  143.8 1.0 fusion.203
  144.8 3.2 %collective-permute-start.2 = (f32[2,4096]{1,0:T(2,128)S(1)}, f32[2,4096]{1,0:T(2,128)S(1)}, u32[]{:S(2)}, u32[]{:S(2)}) collective-permute-start(f32[2,4096]{1,0:T(2,128)S(1)} %get-tuple-element.13), channel_id=1, source_target_pairs={{0,16},{16,32},{32,48},{48,64},{64,80},{80,96},{96,112},{1,17},{17... | collective-permute-start | bytes 98312 | tf_op jit(solution)/shard_map/ppermute | solution.py:15
  148.0 1.3 collective-permute-start.3
  149.3 0.0 collective-permute-done.2
  149.3 3.3 %collective-permute-done.3 = f32[2,4096]{1,0:T(2,128)S(1)} collective-permute-done((f32[2,4096]{1,0:T(2,128)S(1)}, f32[2,4096]{1,0:T(2,128)S(1)}, u32[]{:S(2)}, u32[]{:S(2)}) %collective-permute-start.3) | collective-permute-done | bytes 32800 | tf_op jit(solution)/shard_map/ppermute | solution.py:17
  152.6 11.0 %select_maximum_fusion = f32[520,4104]{1,0:T(8,128)S(1)} fusion(f32[2,4096]{1,0:T(2,128)S(1)} %collective-permute-done.3, f32[512,4096]{1,0:T(8,128)} %param.6, f32[2,4096]{1,0:T(2,128)S(1)} %collective-permute-done.2), kind=kLoop, calls=%fused_computation.2 | loop fusion | flops 27743040 | bytes 16990464 | tf_op jit(solution)/shard_map/concatenate | solution.py:13
  163.7 3.3 %fusion.202 = (f32[520,520]{1,0:T(8,128)S(1)}, f32[520,520]{1,0:T(8,128)S(1)}, f32[520,520]{1,0:T(8,128)}, f32[520,520]{1,0:T(8,128)}, f32[520,520]{1,0:T(8,128)...) fusion(f32[520,4104]{1,0:T(8,128)S(1)} %select_maximum_fusion), kind=kLoop, calls=%fused_computation.223 | loop fusion | bytes 17305600 | tf_op jit(solution)/shard_map/slice | solution.py:66
  167.0 11.6 %concatenate.14 = f32[520,4160]{1,0:T(8,128)} concatenate(f32[520,520]{1,0:T(8,128)} %get-tuple-element.12, f32[520,520]{1,0:T(8,128)} %get-tuple-element.11, f32[520,520]{1,0:T(8,128)} %get-tuple-element.10, f32[520,520]{1,0:T(8,128)} %get-tuple-element.9, f32[520,520]{1,0:T(8,128)} %get-tuple-element.8, f32[520,520]{1,0:T(8,128)} %get-tuple-element.7, ...), dimensions={1} | concatenate | bytes 17305600 | tf_op jit(solution)/shard_map/concatenate | solution.py:66
  178.6 73.8 %all-gather.5.cloned.1.call-done = f32[2,4160,256]{2,1,0:T(8,128)} async-done(((f32[2,520,256]{2,1,0:T(8,128)}), f32[2,4160,256]{2,1,0:T(8,128)}) %all-gather.5.cloned.1.call-update) | async-done | bytes 8519696 | tf_op jit(solution)/shard_map/all_gather | solution.py:86
  252.4 12.2 %fusion.26 = f32[2,520,256]{2,1,0:T(8,128)S(1)} fusion(f32[2,4160,256]{2,1,0:T(8,128)} %all-gather.5.cloned.1.call-done, f32[520,4160]{1,0:T(8,128)} %concatenate.14), kind=kOutput, calls=%fused_computation.53 | convolution fusion | flops 6645350400 | bytes 18237440 | tf_op jit(solution)/shard_map/ik,rkj->rij/dot_general | solution.py:85
  264.6 0.2 fusion.205
  264.8 0.2 copy.24
  265.0 3.2 %collective-permute-start.4 = (f32[2,520,2]{1,2,0:T(2,128)S(1)}, f32[2,520,2]{1,2,0:T(2,128)S(1)}, u32[]{:S(2)}, u32[]{:S(2)}) collective-permute-start(f32[2,520,2]{1,2,0:T(2,128)S(1)} %copy.24), channel_id=1, source_target_pairs={{0,1},{1,2},{2,3},{3,4},{4,5},{5,6},{6,7},{7,8},{8,9},{9,10},{10,1... | collective-permute-start | bytes 24968 | tf_op jit(solution)/shard_map/ppermute | solution.py:15
  268.2 0.2 copy.25
  268.4 2.1 collective-permute-start.5
  270.6 0.0 collective-permute-done.4
  270.6 0.2 copy.26
  270.8 2.6 collective-permute-done.5
  273.4 0.2 copy.27
  273.7 2.8 fusion.37
  276.5 2.9 fusion.35
  279.3 2.6 add_add_fusion
  281.9 1.7 fusion.31
  283.6 0.0 copy-start
  283.6 0.0 copy-start.1
  283.6 1.7 fusion.32
  285.3 0.5 copy-done
  285.8 0.7 copy-done.1
  286.5 4.6 %multiply_add_fusion = f32[2,1024,512]{2,1,0:T(8,128)} fusion(f32[2,1024,512]{2,1,0:T(8,128)S(1)} %copy-done, f32[2,1024,512]{2,1,0:T(8,128)S(1)} %fusion.31, f32[2,1024,512]{2,1,0:T(8,128)S(1)} %fusion.32, f32[1024,512]{1,0:T(8,128)S(1)} %copy-done.1, f32[2,260,1024]{2,1,0:T(8,128)S(1)} %add_add_fusion, f32[512]{0:T(512)S(1)} %multiply_add_fusion.3, ...), kind=kOutput, calls=%fused_computation.17 | convolution fusion | flops 554512384 | bytes 21007376 | tf_op jit(solution)/shard_map/rpj,jq->rpq/dot_general | solution.py:57
  (5 shorter events, 0.0 us)
Async XLA Ops:
  6.5 124.7 %all-gather.3.cloned.1.call-start = ((), (), s32[]{:S(2)}) async-start(), calls=%async_computation | async-start | bytes 18104320 | tf_op jit(solution)/shard_map/all_gather | solution.py:83
  12.8 6.6 %collective-permute-start = (f32[2,1024,4]{1,2,0:T(4,128)S(1)}, f32[2,1024,4]{1,2,0:T(4,128)S(1)}, u32[]{:S(2)}, u32[]{:S(2)}) collective-permute-start(f32[2,1024,4]{1,2,0:T(4,128)S(1)} %get-tuple-element.15), channel_id=1, source_target_pairs={{0,1},{1,2},{2,3},{3,4},{4,5},{5,6},{6,7},{7,8},{8,9},{9,10},{10,1... | collective-permute-start | bytes 98312 | tf_op jit(solution)/shard_map/ppermute | solution.py:15
  17.4 5.2 %collective-permute-start.1 = (f32[2,1024,4]{1,2,0:T(4,128)S(1)}, f32[2,1024,4]{1,2,0:T(4,128)S(1)}, u32[]{:S(2)}, u32[]{:S(2)}) collective-permute-start(f32[2,1024,4]{1,2,0:T(4,128)S(1)} %get-tuple-element.16), channel_id=1, source_target_pairs={{1,0},{2,1},{3,2},{4,3},{5,4},{6,5},{7,6},{8,7},{9,8},{10,9},{11,1... | collective-permute-start | bytes 98312 | tf_op jit(solution)/shard_map/ppermute | solution.py:17
  19.3 7.1 %copy-start.2 = (f32[2,1024,512]{1,2,0:T(8,128)S(1)}, f32[2,1024,512]{1,2,0:T(8,128)}, u32[]{:S(2)}) copy-start(f32[2,1024,512]{1,2,0:T(8,128)} %copy.21) | copy-start | bytes 12582916
  35.5 216.9 %all-gather.5.cloned.1.call-start = ((), (), s32[]{:S(2)}) async-start(), calls=%async_computation.1 | async-start | bytes 9584640 | tf_op jit(solution)/shard_map/all_gather | solution.py:86
  144.8 4.5 %collective-permute-start.2 = (f32[2,4096]{1,0:T(2,128)S(1)}, f32[2,4096]{1,0:T(2,128)S(1)}, u32[]{:S(2)}, u32[]{:S(2)}) collective-permute-start(f32[2,4096]{1,0:T(2,128)S(1)} %get-tuple-element.13), channel_id=1, source_target_pairs={{0,16},{16,32},{32,48},{48,64},{64,80},{80,96},{96,112},{1,17},{17... | collective-permute-start | bytes 98312 | tf_op jit(solution)/shard_map/ppermute | solution.py:15
  148.0 4.7 %collective-permute-start.3 = (f32[2,4096]{1,0:T(2,128)S(1)}, f32[2,4096]{1,0:T(2,128)S(1)}, u32[]{:S(2)}, u32[]{:S(2)}) collective-permute-start(f32[2,4096]{1,0:T(2,128)S(1)} %get-tuple-element.14), channel_id=1, source_target_pairs={{16,0},{32,16},{48,32},{64,48},{80,64},{96,80},{112,96},{17,1},{33... | collective-permute-start | bytes 98312 | tf_op jit(solution)/shard_map/ppermute | solution.py:17
  265.0 5.6 %collective-permute-start.4 = (f32[2,520,2]{1,2,0:T(2,128)S(1)}, f32[2,520,2]{1,2,0:T(2,128)S(1)}, u32[]{:S(2)}, u32[]{:S(2)}) collective-permute-start(f32[2,520,2]{1,2,0:T(2,128)S(1)} %copy.24), channel_id=1, source_target_pairs={{0,1},{1,2},{2,3},{3,4},{4,5},{5,6},{6,7},{7,8},{8,9},{9,10},{10,1... | collective-permute-start | bytes 24968 | tf_op jit(solution)/shard_map/ppermute | solution.py:15
  268.4 5.0 %collective-permute-start.5 = (f32[2,520,2]{1,2,0:T(2,128)S(1)}, f32[2,520,2]{1,2,0:T(2,128)S(1)}, u32[]{:S(2)}, u32[]{:S(2)}) collective-permute-start(f32[2,520,2]{1,2,0:T(2,128)S(1)} %copy.25), channel_id=1, source_target_pairs={{1,0},{2,1},{3,2},{4,3},{5,4},{6,5},{7,6},{8,7},{9,8},{10,9},{11,1... | collective-permute-start | bytes 24968 | tf_op jit(solution)/shard_map/ppermute | solution.py:17
  283.6 2.2 copy-start
  283.6 2.9 copy-start.1
Sparse Core Ops, SparseCore 0:
  35.6 95.5 all-gather.2
  143.9 108.4 all-gather.4
